TPU v7x, 512 devices: a whole 4x8x8 slice. The times are simulated.
512 devices in a mesh: seq: 32 (over x, z_lo, core), tp: 16 (over y, z_hi).
Axes of the slice: x: 4, y: 8, z: 8 (z_hi: 2, z_lo: 4; z = z_hi * 4 + z_lo), core: 2. Of those that a mesh axis runs over, the one named last changes fastest.
Arguments:
- q_in: bfloat16 [16384, 4096], P('seq', 'tp'), may hold values from -40 to 40
- k_in: bfloat16 [16384, 4096], P('seq', 'tp'), may hold values from -40 to 40
- v_in: bfloat16 [16384, 4096], P('seq', 'tp'), may hold values from -6 to 6
- q_gain: float32 [4096], P('tp'), may hold values from 0.1 to 1.9
- k_gain: float32 [4096], P('tp'), may hold values from 0.1 to 1.9
- d_out: bfloat16 [16384, 4096], P('seq', 'tp'), may hold values from -6 to 6
- counts: int32 [64], replicated, may hold values from 128 to 256, as said below
- windows: int32 [32], P('tp'), may hold values from 1 to 2
Outputs:
- attn_out: bfloat16 [16384, 4096], P('seq', 'tp')
- grad_q: bfloat16 [16384, 4096], P('seq', 'tp')
- grad_k: bfloat16 [16384, 4096], P('seq', 'tp')
- grad_v: bfloat16 [16384, 4096], P('seq', 'tp')
Inputs may be any that keep to these rules, and one draw needn't show every extreme that they name: `counts`: each count is a multiple of 128; slots at or beyond a frame's count are padding; some frame is full.
All inputs are finite; a program needn't handle non-finite values.
Results may differ from a plain program's by a relative error of at most 0.02.
The roundings to bfloat16 on the way count: a program that leaves them out, or rounds other values in their place, can miss the bound.
Values may be sent and summed in bfloat16 or wider, within the bound.
No kernel may reach another device: no remote copies, remote signals or barrier semaphores. Data moves between devices by JAX's collectives and lax.ppermute only.
A program may use at most 64 MiB of HBM per device.

v0:
```python
import jax
import jax.numpy as jnp
from jax import lax
from jax.sharding import PartitionSpec as P

HD = 128
CAP = 256
F_DEV = 2
WIDTH = 4096
EPS = 1e-06
NEG = -1e30


def shifted(block, axis, distance):
    devices = range(lax.axis_size(axis))
    route = [(i - distance, i) for i in devices if i - distance in devices]
    return lax.ppermute(block, axis, route)


def from_root(x, axis, root):
    mine = lax.axis_index(axis) == root
    return lax.psum(jnp.where(mine, x, jnp.zeros_like(x)), axis)


def stack_offsets(padded, before, count):
    blocks = [padded[before - offset : before - offset + count] for offset in range(before + 1)]
    return jnp.concatenate(blocks, axis=1)


def fold_offsets(grads, before, count, slots):
    result = jnp.zeros((before + count, slots) + grads.shape[2:], jnp.float32)
    for offset in range(before + 1):
        piece = grads[:, offset * slots : (offset + 1) * slots]
        result = result + jnp.pad(piece, ((before - offset, offset), (0, 0), (0, 0)))
    return result


def attend(q_head, g_head, k_set, v_set, visible, row_live):
    factor = HD ** (-0.5)
    scores = jnp.einsum("fqd,fkd->fqk", q_head, k_set, preferred_element_type=jnp.float32) * factor
    scores = jnp.where(visible[:, None, :], scores, NEG)
    row_max = jnp.max(scores, axis=2, keepdims=True)
    row_sum = jnp.sum(jnp.exp(scores - row_max), axis=2, keepdims=True)
    lse = row_max + jnp.log(row_sum)
    prob_wide = jnp.exp(scores - lse)
    prob = prob_wide.astype(jnp.bfloat16)
    out_wide = jnp.einsum("fqk,fkd->fqd", prob, v_set, preferred_element_type=jnp.float32)
    attn = lax.optimization_barrier(
        jnp.where(row_live[:, :, None], out_wide, 0.0).astype(jnp.bfloat16)
    )
    delta = jnp.sum(g_head.astype(jnp.float32) * attn.astype(jnp.float32), axis=2)
    dprob = jnp.einsum("fqd,fkd->fqk", g_head, v_set, preferred_element_type=jnp.float32)
    dscore = (prob_wide * (dprob - delta[:, :, None]) * factor).astype(jnp.bfloat16)
    grad_qh = jnp.einsum("fqk,fkd->fqd", dscore, k_set, preferred_element_type=jnp.float32)
    grad_kh = jnp.einsum("fqk,fqd->fkd", dscore, q_head, preferred_element_type=jnp.float32)
    grad_vh = jnp.einsum("fqk,fqd->fkd", prob, g_head, preferred_element_type=jnp.float32)
    return (attn, lse[:, :, 0], delta, grad_qh, grad_kh, grad_vh)


def on_device(q_in, k_in, v_in, q_gain, k_gain, d_out, counts, windows):
    row_count, local_width = q_in.shape
    local_heads = local_width // HD
    device = lax.axis_index("seq")
    q_float = q_in.astype(jnp.float32)
    k_float = k_in.astype(jnp.float32)
    q_power, k_power = lax.psum(
        (jnp.sum(q_float * q_float, axis=1), jnp.sum(k_float * k_float, axis=1)), "tp"
    )
    q_rinv = lax.rsqrt(q_power / WIDTH + EPS)[:, None]
    k_rinv = lax.rsqrt(k_power / WIDTH + EPS)[:, None]
    q_norm = (q_float * q_rinv * q_gain).astype(jnp.bfloat16)
    k_norm = (k_float * k_rinv * k_gain).astype(jnp.bfloat16)
    padded_counts = jnp.concatenate([jnp.zeros((F_DEV,), jnp.int32), counts])
    near_counts = lax.dynamic_slice_in_dim(padded_counts, device * F_DEV, 2 * F_DEV)
    slot_index = jnp.arange(CAP, dtype=jnp.int32)
    near_live = slot_index[None, :] < near_counts[:, None]
    row_live = near_live[F_DEV:]
    grad_mask = jnp.where(row_live.reshape(row_count)[:, None], d_out, jnp.zeros_like(d_out))
    halo_k, halo_v = shifted((k_norm, v_in), "seq", 1)
    anchor_k, anchor_v = (from_root(k_norm[:CAP], "seq", 0), from_root(v_in[:CAP], "seq", 0))
    k_near = jnp.concatenate([halo_k, k_norm], axis=0).reshape(2 * F_DEV, CAP, local_width)
    v_near = jnp.concatenate([halo_v, v_in], axis=0).reshape(2 * F_DEV, CAP, local_width)
    k_set = jnp.concatenate(
        [
            stack_offsets(k_near, F_DEV, F_DEV),
            jnp.broadcast_to(anchor_k[None], (F_DEV, CAP, local_width)),
        ],
        axis=1,
    )
    v_set = jnp.concatenate(
        [
            stack_offsets(v_near, F_DEV, F_DEV),
            jnp.broadcast_to(anchor_v[None], (F_DEV, CAP, local_width)),
        ],
        axis=1,
    )

    def to_heads(value):
        return value.reshape(value.shape[0], value.shape[1], local_heads, HD).transpose(2, 0, 1, 3)

    def from_heads(value):
        return value.transpose(1, 2, 0, 3).reshape(value.shape[1], value.shape[2], local_heads * HD)

    frame_local = jnp.arange(F_DEV, dtype=jnp.int32)
    offsets = jnp.arange((F_DEV + 1) * CAP, dtype=jnp.int32) // CAP
    live_stack = stack_offsets(near_live[:, :, None], F_DEV, F_DEV)[:, :, 0]
    reach = device * F_DEV + frame_local[:, None] - offsets[None, :] >= 0
    within = offsets[None, None, :] <= windows[:, None, None]
    anchor_ok = device * F_DEV + frame_local[None, :] - windows[:, None] > 0
    anchor_live = slot_index < counts[0]
    visible = jnp.concatenate(
        [(live_stack & reach)[None] & within, anchor_ok[:, :, None] & anchor_live[None, None, :]],
        axis=2,
    )

    def per_head(items):
        q_head, g_head, k_head, v_head, seen = items
        return attend(q_head, g_head, k_head, v_head, seen, row_live)

    q_heads = to_heads(q_norm.reshape(F_DEV, CAP, local_width))
    g_heads = to_heads(grad_mask.reshape(F_DEV, CAP, local_width))
    attn_h, lse_h, delta_h, grad_qh, grad_kh, grad_vh = lax.map(
        per_head, (q_heads, g_heads, to_heads(k_set), to_heads(v_set), visible)
    )
    attn_out = from_heads(attn_h).reshape(row_count, local_width)
    grad_qn = from_heads(grad_qh).reshape(row_count, local_width)
    grad_k_all = from_heads(grad_kh)
    grad_v_all = from_heads(grad_vh)
    split = (F_DEV + 1) * CAP
    grad_k_near = fold_offsets(grad_k_all[:, :split], F_DEV, F_DEV, CAP)
    grad_v_near = fold_offsets(grad_v_all[:, :split], F_DEV, F_DEV, CAP)
    grad_k_anchor = jnp.sum(grad_k_all[:, split:], axis=0)
    grad_v_anchor = jnp.sum(grad_v_all[:, split:], axis=0)
    back_k, back_v = shifted((grad_k_near[:F_DEV], grad_v_near[:F_DEV]), "seq", -1)
    grad_k_own = grad_k_near[F_DEV:] + back_k
    grad_v_own = grad_v_near[F_DEV:] + back_v
    anchor_gk, anchor_gv = lax.psum((grad_k_anchor, grad_v_anchor), "seq")
    first_device = device == 0
    grad_k_own = grad_k_own.at[0].add(jnp.where(first_device, anchor_gk, 0.0))
    grad_v_own = grad_v_own.at[0].add(jnp.where(first_device, anchor_gv, 0.0))
    q_scaled = grad_qn * q_gain
    k_scaled = grad_k_own.reshape(row_count, local_width) * k_gain
    q_dot, k_dot = lax.psum(
        (jnp.sum(q_float * q_scaled, axis=1), jnp.sum(k_float * k_scaled, axis=1)), "tp"
    )
    grad_q = (q_rinv * q_scaled - q_float * q_rinv**3 * q_dot[:, None] / WIDTH).astype(jnp.bfloat16)
    grad_k = (k_rinv * k_scaled - k_float * k_rinv**3 * k_dot[:, None] / WIDTH).astype(jnp.bfloat16)
    grad_v = grad_v_own.reshape(row_count, local_width).astype(jnp.bfloat16)
    return (attn_out, grad_q, grad_k, grad_v)


def solution(mesh):
    return jax.shard_map(
        on_device,
        mesh=mesh,
        in_specs=(
            P("seq", "tp"),
            P("seq", "tp"),
            P("seq", "tp"),
            P("tp"),
            P("tp"),
            P("seq", "tp"),
            P(),
            P("tp"),
        ),
        out_specs=(P("seq", "tp"), P("seq", "tp"), P("seq", "tp"), P("seq", "tp")),
        check_vma=False,
    )
```

profile of v0, /device:TPU:8, one launch (start us, length us, event | category | flops | bytes accessed | tf_op | source)
XLA Modules:
  0.0 734.2 jit_solution(7441168945927711885)
XLA Ops:
  7.3 1.2 fusion.29
  8.5 1.1 fusion.37
  9.6 56.1 %all-reduce.9 = (f32[512]{0:T(512)S(1)}, f32[512]{0:T(512)S(1)}) all-reduce(f32[512]{0:T(512)S(1)} %fusion.29, f32[512]{0:T(512)S(1)} %fusion.37), channel_id=1, replica_groups=mesh['seq'=32,'tp'=16] {'tp'}, use_global_device_ids=true, to_apply=%region_1.0 | all-reduce | flops 1024 | bytes 8192 | tf_op jit(solution)/shard_map/psum | solution.py:66
  65.6 1.1 fusion.39
  66.7 1.3 collective-permute-start
  68.1 4.0 collective-permute-start.1
  75.8 280.9 %all-reduce.16.cloned.1.call-done = (bf16[256,2,128]{2,1,0:T(2,128)(2,1)}, bf16[256,2,128]{2,1,0:T(2,128)(2,1)}) async-done(((bf16[256,2,128]{2,1,0:T(2,128)(2,1)}, bf16[256,2,128]{2,1,0:T(2,128)(2,1)}), (bf16[256,2,128]{2,1,0:T(2,128)(2,1)}, bf16[256,2,128]{2,1,0:T(2,128)(2,1)})) %all-reduce.16.cloned.1.call-update) | async-done | bytes 262160 | tf_op jit(solution)/shard_map/psum | solution.py:22
  359.7 1.6 maximum_bitcast_fusion.1
  361.5 17.1 %while.18 = (s32[]{:T(128)}, bf16[2,2,256,128]{3,2,1,0:T(8,128)(2,1)}, f32[2,2,256,128]{3,2,1,0:T(8,128)}, f32[2,2,1024,128]{3,2,1,0:T(8,128)}, f32[2,2,1024,128...) while((s32[]{:T(128)}, ...), condition=%wide.region_10.11_spmd, body=%wide.region_6.10_spmd.sunk | while | flops 813038592 | bytes 57053992 | solution.py:122
  363.9 1.3 copy-done.6
  372.4 1.3 copy-done.6
  378.6 1.7 copy_bitcast_fusion
  382.1 1.3 collective-permute-start.3
  383.6 1.6 slice_reduce_fusion.1
  385.3 1.2 pad_add_fusion.1
  387.3 1.3 collective-permute-start.2
  389.2 1.2 copy.33
  391.2 1.1 slice_add_fusion
  392.3 277.9 %all-reduce.14.cloned.1.call-done = (f32[256,256]{1,0:T(8,128)}, f32[256,256]{1,0:T(8,128)}) async-done(((f32[256,256]{1,0:T(8,128)}, f32[256,256]{1,0:T(8,128)}), (f32[256,256]{1,0:T(8,128)}, f32[256,256]{1,0:T(8,128)})) %all-reduce.14.cloned.1.call-update) | async-done | bytes 524304 | tf_op jit(solution)/shard_map/psum | solution.py:137
  670.2 1.1 fusion.45
  672.0 1.1 slice_add_fusion.1
  673.3 52.0 %all-reduce.8 = (f32[512]{0:T(512)S(1)}, f32[512]{0:T(512)S(1)}) all-reduce(f32[512]{0:T(512)S(1)} %fusion.36, f32[512]{0:T(512)S(1)} %fusion.44), channel_id=1, replica_groups=mesh['seq'=32,'tp'=16] {'tp'}, use_global_device_ids=true, to_apply=%region_12.13 | all-reduce | flops 1024 | bytes 8192 | tf_op jit(solution)/shard_map/psum | solution.py:143
  725.4 1.0 fusion.43
  726.3 1.0 fusion.35
  (134 shorter events, 26.0 us)
Async XLA Ops:
  7.2 67.9 %copy-start.1 = (bf16[512,256]{1,0:T(8,128)(2,1)S(1)}, bf16[512,256]{1,0:T(8,128)(2,1)}, u32[]{:S(2)}) copy-start(bf16[512,256]{1,0:T(8,128)(2,1)} %param.14) | copy-start | bytes 786436
  7.2 68.2 %copy-start.7 = (bf16[512,256]{1,0:T(8,128)(2,1)S(1)}, bf16[512,256]{1,0:T(8,128)(2,1)}, u32[]{:S(2)}) copy-start(bf16[512,256]{1,0:T(8,128)(2,1)} %param.16) | copy-start | bytes 786436
  7.2 67.3 %copy-start.19 = (s32[64]{0:T(128)S(1)}, s32[64]{0:T(128)}, u32[]{:S(2)}) copy-start(s32[64]{0:T(128)} %param.20) | copy-start | bytes 772
  7.2 67.6 %copy-start.18 = (s32[2]{0:T(128)S(1)}, s32[2]{0:T(128)}, u32[]{:S(2)}) copy-start(s32[2]{0:T(128)} %param.21) | copy-start | bytes 28
  7.2 67.7 %copy-start.13 = (bf16[512,256]{1,0:T(8,128)(2,1)S(1)}, bf16[512,256]{1,0:T(8,128)(2,1)}, u32[]{:S(2)}) copy-start(bf16[512,256]{1,0:T(8,128)(2,1)} %param.19) | copy-start | bytes 786436
  7.2 67.9 %copy-start.17 = (f32[256]{0:T(256)S(1)}, f32[256]{0:T(256)}, u32[]{:S(2)}) copy-start(f32[256]{0:T(256)} %param.17) | copy-start | bytes 3076
  7.2 349.5 %all-reduce.16.cloned.1.call-start = ((), (), s32[]{:S(2)}) async-start(), calls=%async_computation.1 | async-start | bytes 524288 | tf_op jit(solution)/shard_map/psum | solution.py:22
  66.7 290.9 %collective-permute-start = (bf16[512,256]{1,0:T(8,128)(2,1)S(1)}, bf16[512,256]{1,0:T(8,128)(2,1)S(1)}, u32[]{:S(2)}, u32[]{:S(2)}) collective-permute-start(bf16[512,256]{1,0:T(8,128)(2,1)S(1)} %fusion.39), channel_id=1, source_target_pairs={{0,16},{16,32},{32,48},{48,64},{64,80},{80,96},{96,112},{112,128},... | collective-permute-start | bytes 786440 | tf_op jit(solution)/shard_map/ppermute | solution.py:17
  68.1 291.3 %collective-permute-start.1 = (bf16[512,256]{1,0:T(8,128)(2,1)}, bf16[512,256]{1,0:T(8,128)(2,1)S(1)}, u32[]{:S(2)}, u32[]{:S(2)}) collective-permute-start(bf16[512,256]{1,0:T(8,128)(2,1)} %param.16), channel_id=1, source_target_pairs={{0,16},{16,32},{32,48},{48,64},{64,80},{80,96},{96,112},{112,128},... | collective-permute-start | bytes 786440 | tf_op jit(solution)/shard_map/ppermute | solution.py:17
  74.4 595.7 %all-reduce.14.cloned.1.call-start = ((), (), s32[]{:S(2)}) async-start(), calls=%async_computation | async-start | bytes 1048576 | tf_op jit(solution)/shard_map/psum | solution.py:137
  357.7 1.8 copy-start.15
  359.6 1.8 copy-start.8
  359.7 1.8 copy-start.9
  361.6 1.6 copy-start.5
  365.8 1.6 copy-start.2
  365.9 2.0 copy-start.10
  374.4 2.0 copy-start.10
  381.2 2.2 copy-start.4
  382.1 9.0 %collective-permute-start.3 = (f32[2,256,256]{2,1,0:T(8,128)}, f32[2,256,256]{2,1,0:T(8,128)}, u32[]{:S(2)}, u32[]{:S(2)}) collective-permute-start(f32[2,256,256]{2,1,0:T(8,128)} %slice.172), channel_id=1, source_target_pairs={{16,0},{32,16},{48,32},{64,48},{80,64},{96,80},{112,96},{128,112},... | collective-permute-start | bytes 1572872 | tf_op jit(solution)/shard_map/ppermute | solution.py:17
  385.3 3.3 copy-start.12
  387.3 284.6 %collective-permute-start.2 = (f32[2,256,256]{2,1,0:T(8,128)}, f32[2,256,256]{2,1,0:T(8,128)}, u32[]{:S(2)}, u32[]{:S(2)}) collective-permute-start(f32[2,256,256]{2,1,0:T(8,128)} %slice.165), channel_id=1, source_target_pairs={{16,0},{32,16},{48,32},{64,48},{80,64},{96,80},{112,96},{128,112},... | collective-permute-start | bytes 1572872 | tf_op jit(solution)/shard_map/ppermute | solution.py:17
  392.3 280.9 %copy-start = (bf16[512,256]{1,0:T(8,128)(2,1)S(1)}, bf16[512,256]{1,0:T(8,128)(2,1)}, u32[]{:S(2)}) copy-start(bf16[512,256]{1,0:T(8,128)(2,1)} %param.15) | copy-start | bytes 786436
  392.3 280.9 %copy-start.16 = (f32[256]{0:T(256)S(1)}, f32[256]{0:T(256)}, u32[]{:S(2)}) copy-start(f32[256]{0:T(256)} %param.18) | copy-start | bytes 3076
  670.2 2.9 copy-start.14
  (8 other events, 10.2 us)
Sparse Core Ops, SparseCore 0:
  74.6 282.1 all-reduce.15
  385.4 284.7 all-reduce.13
where the time goes:
time: 735 us; the launch traced here: 734 us
  waiting for transfers between devices  559 us (76%)
  blocking collectives  108 us (15%)
  local copies, waits for them, and re-layouts  19.6 us (3%)
  other arithmetic  18.1 us (2%)
  between operations  14.6 us (2%)
  starting transfers between devices  7.95 us (1%)
    psum x1, waiting for transfers between devices, from_root(): return lax.psum(jnp.where(mine, x, jnp.zeros_like(x)), axis)  281 us
    psum x1, waiting for transfers between devices, on_device(): anchor_gk, anchor_gv = lax.psum((grad_k_anchor, grad_v_anchor), 'seq')  278 us
    psum x1, blocking collectives, on_device(): lax.psum((jnp.sum(q_float * q_float, axis=1), jnp.sum(k_float * k_float,...  56.1 us
    psum x1, blocking collectives, on_device(): lax.psum((jnp.sum(q_float * q_scaled, axis=1), jnp.sum(k_float * k_scaled...  52 us
  transfers between devices with their start and end apart: 6, of which 2 were waited for; matrix products, arithmetic and copies ran while one was open for 2% of the time, Pallas kernels for 0%

commit v1 on v0

--- a/solution.py
+++ b/solution.py
@@ -19,7 +19,7 @@
 
 def from_root(x, axis, root):
     mine = lax.axis_index(axis) == root
-    return lax.psum(jnp.where(mine, x, jnp.zeros_like(x)), axis)
+    return jnp.sum(lax.all_gather(jnp.where(mine, x, jnp.zeros_like(x)), axis), axis=0)
 
 
 def stack_offsets(padded, before, count):

time: 735 us -> 578 us (0.79)
  waiting for transfers between devices: 559 us -> 395 us
  other arithmetic: 18.1 us -> 26.9 us
    psum x1 -> x0, waiting for transfers between devices: 281 us -> none  [from_root(): return lax.psum(jnp.where(mine, x, jnp.zeros_like(x)), axis)]
    all_gather x0 -> x2, waiting for transfers between devices: none -> 114 us  [from_root(): lax.all_gather(jnp.where(mine, x, jnp.zeros_like(x)), axis)]
  transfers between devices with their start and end apart: 6 -> 7, of which waited for: 2 -> 3; matrix products, arithmetic and copies ran while one was open for 2% -> 3% of each run, Pallas kernels for 0% -> 0%
where the time goes in v1:
time: 578 us; the launch traced here: 577 us
  waiting for transfers between devices  395 us (68%)
  blocking collectives  108 us (19%)
  other arithmetic  26.9 us (5%)
  local copies, waits for them, and re-layouts  18.2 us (3%)
  between operations  14.3 us (2%)
  starting transfers between devices  7.99 us (1%)
  matrix products  6.8 us (1%)
    psum x1, waiting for transfers between devices, on_device(): anchor_gk, anchor_gv = lax.psum((grad_k_anchor, grad_v_anchor), 'seq')  281 us
    all_gather x2, waiting for transfers between devices, from_root(): lax.all_gather(jnp.where(mine, x, jnp.zeros_like(x)), axis)  114 us
    psum x1, blocking collectives, on_device(): lax.psum((jnp.sum(q_float * q_float, axis=1), jnp.sum(k_float * k_float,...  56.1 us
    psum x1, blocking collectives, on_device(): lax.psum((jnp.sum(q_float * q_scaled, axis=1), jnp.sum(k_float * k_scaled...  52 us
  transfers between devices with their start and end apart: 7, of which 3 were waited for; matrix products, arithmetic and copies ran while one was open for 3% of the time, Pallas kernels for 0%

profile of v1, /device:TPU:8, one launch (start us, length us, event | category | flops | bytes accessed | tf_op | source)
XLA Modules:
  0.0 577.4 jit_solution(4119475487103086638)
XLA Ops:
  7.3 1.2 fusion.29
  8.4 1.1 fusion.37
  9.5 56.1 %all-reduce.9 = (f32[512]{0:T(512)S(1)}, f32[512]{0:T(512)S(1)}) all-reduce(f32[512]{0:T(512)S(1)} %fusion.29, f32[512]{0:T(512)S(1)} %fusion.37), channel_id=1, replica_groups=mesh['seq'=32,'tp'=16] {'tp'}, use_global_device_ids=true, to_apply=%region_1.0 | all-reduce | flops 1024 | bytes 8192 | tf_op jit(solution)/shard_map/psum | solution.py:66
  65.6 1.1 fusion.39
  67.4 1.6 slice_select_fusion.1
  69.1 1.3 collective-permute-start
  70.4 4.0 collective-permute-start.1
  80.1 51.0 %all-gather.5.cloned.1.call-done = bf16[8192,256]{1,0:T(8,128)(2,1)} async-done(((bf16[256,256]{1,0:T(8,128)(2,1)}), bf16[8192,256]{1,0:T(8,128)(2,1)}) %all-gather.5.cloned.1.call-update) | async-done | bytes 4194320 | tf_op jit(solution)/shard_map/all_gather | solution.py:22
  131.1 2.8 reduce_sum.98
  134.1 63.3 %all-gather.7.cloned.1.call-done = bf16[8192,256]{1,0:T(8,128)(2,1)} async-done(((bf16[256,256]{1,0:T(8,128)(2,1)}), bf16[8192,256]{1,0:T(8,128)(2,1)}) %all-gather.7.cloned.1.call-update) | async-done | bytes 4194320 | tf_op jit(solution)/shard_map/all_gather | solution.py:22
  197.4 2.8 reduce_sum.99
  200.6 1.6 maximum_bitcast_fusion.1
  203.2 17.1 %while.18 = (s32[]{:T(128)}, bf16[2,2,256,128]{3,2,1,0:T(8,128)(2,1)S(1)}, f32[2,2,256,128]{3,2,1,0:T(8,128)}, f32[2,2,1024,128]{3,2,1,0:T(8,128)}, f32[2,2,1024...) while((s32[]{:T(128)}, ...), condition=%wide.region_10.11_spmd, body=%wide.region_6.10_spmd.sunk | while | flops 813038592 | bytes 57053484 | solution.py:122
  205.5 1.3 copy-done.6
  214.1 1.3 copy-done.6
  220.3 1.8 copy_bitcast_fusion
  223.9 1.3 collective-permute-start.3
  225.4 1.6 slice_reduce_fusion.1
  227.1 1.2 pad_add_fusion.1
  229.1 1.3 collective-permute-start.2
  232.0 1.1 slice_add_fusion
  233.2 280.5 %all-reduce.12.cloned.1.call-done = (f32[256,256]{1,0:T(8,128)}, f32[256,256]{1,0:T(8,128)}) async-done(((f32[256,256]{1,0:T(8,128)}, f32[256,256]{1,0:T(8,128)}), (f32[256,256]{1,0:T(8,128)}, f32[256,256]{1,0:T(8,128)})) %all-reduce.12.cloned.1.call-update) | async-done | bytes 524304 | tf_op jit(solution)/shard_map/psum | solution.py:137
  515.5 1.1 slice_add_fusion.1
  516.9 52.0 %all-reduce.8 = (f32[512]{0:T(512)S(1)}, f32[512]{0:T(512)S(1)}) all-reduce(f32[512]{0:T(512)S(1)} %fusion.36, f32[512]{0:T(512)S(1)} %fusion.44), channel_id=1, replica_groups=mesh['seq'=32,'tp'=16] {'tp'}, use_global_device_ids=true, to_apply=%region_12.13 | all-reduce | flops 1024 | bytes 8192 | tf_op jit(solution)/shard_map/psum | solution.py:143
  (140 shorter events, 30.5 us)
Async XLA Ops:
  7.2 70.4 %copy-start.1 = (bf16[512,256]{1,0:T(8,128)(2,1)S(1)}, bf16[512,256]{1,0:T(8,128)(2,1)}, u32[]{:S(2)}) copy-start(bf16[512,256]{1,0:T(8,128)(2,1)} %param.14) | copy-start | bytes 786436
  7.2 70.7 %copy-start.7 = (bf16[512,256]{1,0:T(8,128)(2,1)S(1)}, bf16[512,256]{1,0:T(8,128)(2,1)}, u32[]{:S(2)}) copy-start(bf16[512,256]{1,0:T(8,128)(2,1)} %param.16) | copy-start | bytes 786436
  7.2 70.2 %copy-start.13 = (bf16[512,256]{1,0:T(8,128)(2,1)S(1)}, bf16[512,256]{1,0:T(8,128)(2,1)}, u32[]{:S(2)}) copy-start(bf16[512,256]{1,0:T(8,128)(2,1)} %param.19) | copy-start | bytes 786436
  7.2 70.4 %copy-start.19 = (f32[256]{0:T(256)S(1)}, f32[256]{0:T(256)}, u32[]{:S(2)}) copy-start(f32[256]{0:T(256)} %param.17) | copy-start | bytes 3076
  7.2 123.9 %all-gather.5.cloned.1.call-start = ((), (), s32[]{:S(2)}) async-start(), calls=%async_computation | async-start | bytes 4325376 | tf_op jit(solution)/shard_map/all_gather | solution.py:22
  67.4 130.0 %all-gather.7.cloned.1.call-start = ((), (), s32[]{:S(2)}) async-start(), calls=%async_computation.1 | async-start | bytes 4325376 | tf_op jit(solution)/shard_map/all_gather | solution.py:22
  69.0 444.7 %all-reduce.12.cloned.1.call-start = ((), (), s32[]{:S(2)}) async-start(), calls=%async_computation.2 | async-start | bytes 1048576 | tf_op jit(solution)/shard_map/psum | solution.py:137
  69.1 9.2 %collective-permute-start = (bf16[512,256]{1,0:T(8,128)(2,1)S(1)}, bf16[512,256]{1,0:T(8,128)(2,1)S(1)}, u32[]{:S(2)}, u32[]{:S(2)}) collective-permute-start(bf16[512,256]{1,0:T(8,128)(2,1)S(1)} %fusion.39), channel_id=1, source_target_pairs={{0,16},{16,32},{32,48},{48,64},{64,80},{80,96},{96,112},{112,128},... | collective-permute-start | bytes 786440 | tf_op jit(solution)/shard_map/ppermute | solution.py:17
  70.4 9.6 %collective-permute-start.1 = (bf16[512,256]{1,0:T(8,128)(2,1)}, bf16[512,256]{1,0:T(8,128)(2,1)S(1)}, u32[]{:S(2)}, u32[]{:S(2)}) collective-permute-start(bf16[512,256]{1,0:T(8,128)(2,1)} %param.16), channel_id=1, source_target_pairs={{0,16},{16,32},{32,48},{48,64},{64,80},{80,96},{96,112},{112,128},... | collective-permute-start | bytes 786440 | tf_op jit(solution)/shard_map/ppermute | solution.py:17
  200.6 1.8 copy-start.8
  200.6 1.8 copy-start.9
  207.3 1.6 copy-start.2
  207.5 2.0 copy-start.10
  215.9 1.6 copy-start.2
  216.1 2.0 copy-start.10
  220.3 1.9 copy-start.15
  223.0 2.2 copy-start.4
  223.9 8.1 %collective-permute-start.3 = (f32[2,256,256]{2,1,0:T(8,128)}, f32[2,256,256]{2,1,0:T(8,128)}, u32[]{:S(2)}, u32[]{:S(2)}) collective-permute-start(f32[2,256,256]{2,1,0:T(8,128)} %slice.172), channel_id=1, source_target_pairs={{16,0},{32,16},{48,32},{64,48},{80,64},{96,80},{112,96},{128,112},... | collective-permute-start | bytes 1572872 | tf_op jit(solution)/shard_map/ppermute | solution.py:17
  227.1 3.4 copy-start.12
  228.3 2.7 copy-start.16
  229.1 286.3 %collective-permute-start.2 = (f32[2,256,256]{2,1,0:T(8,128)}, f32[2,256,256]{2,1,0:T(8,128)}, u32[]{:S(2)}, u32[]{:S(2)}) collective-permute-start(f32[2,256,256]{2,1,0:T(8,128)} %slice.165), channel_id=1, source_target_pairs={{16,0},{32,16},{48,32},{64,48},{80,64},{96,80},{112,96},{128,112},... | collective-permute-start | bytes 1572872 | tf_op jit(solution)/shard_map/ppermute | solution.py:17
  233.2 283.5 %copy-start = (bf16[512,256]{1,0:T(8,128)(2,1)S(1)}, bf16[512,256]{1,0:T(8,128)(2,1)}, u32[]{:S(2)}) copy-start(bf16[512,256]{1,0:T(8,128)(2,1)} %param.15) | copy-start | bytes 786436
  233.2 283.5 %copy-start.18 = (f32[256]{0:T(256)S(1)}, f32[256]{0:T(256)}, u32[]{:S(2)}) copy-start(f32[256]{0:T(256)} %param.18) | copy-start | bytes 3076
  513.7 2.9 copy-start.17
  (9 other events, 11.1 us)
Sparse Core Ops, SparseCore 0:
  67.5 63.5 all-gather.4
  133.3 64.1 all-gather.6
  227.2 286.4 all-reduce.11
